TPU v7x, 32 devices: a whole 2x2x4 slice. The times are simulated.
32 devices in a mesh: groups: 2 (over y), blk: 4 (over z), pool: 4 (over x, core).
Axes of the slice: x: 2, y: 2, z: 4, core: 2. Of those that a mesh axis runs over, the one named last changes fastest.
Arguments:
- q_new: bfloat16 [1024, 8192], P(('groups', 'blk'), 'pool'), parts along dimension 0, may hold values from -64 to 64
- kv_new: bfloat16 [1024, 8, 256], P(('groups', 'blk'), 'pool'), parts along dimension 0, may hold values from -7 to 7
- kv_cache: bfloat16 [256, 8, 128, 256], P(('groups', 'blk'), 'pool'), parts along dimension 0, may hold values from -4.5 to 4.5
- page_table: int32 [16], P('groups'), parts along dimension 0, may hold values from 0 to 127, as said below
- block_offsets: int32 [8], P('groups'), parts along dimension 0, may hold values from 0 to 3, each once
Outputs:
- attended: bfloat16 [1024, 8192], P(('groups', 'blk'), 'pool'), parts along dimension 0
There are 2 independent parts, one for each index of `groups`. A program takes and returns all parts, laid end to end along the dimension named above; each array names one. Nothing has to cross between parts.
Inputs may be any that keep to these rules, and one draw needn't show every extreme that they name: `page_table`: distinct slots; slot s lies on blk index s // 32; at most 4 entries lie on the slots of one blk index, and exactly 4 on some blk index.
All inputs are finite; a program needn't handle non-finite values.
Results may differ from a plain program's by a relative error of at most 0.0045.
Values may be sent and summed in bfloat16 or wider, within the bound.
No kernel may reach another device: no remote copies, remote signals or barrier semaphores. Data moves between devices by JAX's collectives and lax.ppermute only.
A program may use at most 64 MiB of HBM per device.

v0:
```python
import math
import jax
import jax.numpy as jnp
from jax import lax
from jax.sharding import PartitionSpec as P

CAP = 4


def attend(running, queries, keys, values, visible, head_size):
    maxima, totals, summed = running
    score_scale = 1.0 / math.sqrt(head_size)
    scores = (
        jnp.einsum("gqd,gkd->gqk", queries, keys, preferred_element_type=jnp.float32) * score_scale
    )
    scores = jnp.where(visible, scores, -1e30)
    row_top = jnp.maximum(maxima, jnp.max(scores, axis=2))
    factor = jnp.exp(maxima - row_top)
    weights = jnp.where(visible, jnp.exp(scores - row_top[..., None]), 0.0)
    totals = totals * factor + jnp.sum(weights, axis=2)
    summed = summed * factor[..., None] + jnp.einsum(
        "gqk,gkd->gqd", weights.astype(jnp.bfloat16), values, preferred_element_type=jnp.float32
    )
    return (row_top, totals, summed)


def local(q_new, kv_new, kv_cache, page_table, block_offsets):
    q_rows = q_new.shape[0]
    kv_heads = kv_new.shape[1]
    head_size = kv_new.shape[2] // 2
    group_size = q_new.shape[1] // (head_size * kv_heads)
    slots_dev = kv_cache.shape[0]
    page_len = kv_cache.shape[2]
    npages = page_table.shape[0]
    blocks = lax.axis_size("blk")
    myself = lax.axis_index("blk")
    pg = -(-npages // blocks)
    block_ids = jnp.arange(blocks, dtype=jnp.int32)
    my_offset = jnp.sum(jnp.where(block_ids == myself, block_offsets, 0))
    query_pos = jnp.tile(my_offset * q_rows + jnp.arange(q_rows, dtype=jnp.int32), group_size)
    queries = (
        q_new.reshape(q_rows, kv_heads, group_size, head_size)
        .transpose(1, 2, 0, 3)
        .reshape(kv_heads, group_size * q_rows, head_size)
    )
    query_span = group_size * q_rows
    page_owner = page_table // slots_dev
    owned = page_owner == myself
    page_rank = jnp.cumsum(owned.astype(jnp.int32)) - 1
    local_slot = page_table % slots_dev
    counts = jnp.sum((page_owner[None, :] == block_ids[:, None]).astype(jnp.int32), axis=1)
    per_peer = (CAP + blocks - 1) // blocks
    starts = jnp.cumsum(counts) - counts
    my_start = jnp.sum(jnp.where(block_ids == myself, starts, 0))
    peer_slots = jnp.arange(per_peer, dtype=jnp.int32)[None, :]
    wanted = (block_ids[:, None] - my_start) % blocks + peer_slots * blocks
    picked = owned[None, None, :] & (page_rank[None, None, :] == wanted[..., None])
    chosen = jnp.sum(jnp.where(picked, local_slot[None, None, :], 0), axis=2).reshape(-1)
    sent_pages = kv_cache[chosen].reshape(blocks, per_peer, kv_heads, page_len, 2 * head_size)
    sent_pages = sent_pages.transpose(0, 2, 1, 3, 4).reshape(
        blocks, kv_heads, per_peer * page_len, 2 * head_size
    )
    own_rows = jnp.broadcast_to(
        kv_new.transpose(1, 0, 2)[None], (blocks, kv_heads, q_rows, 2 * head_size)
    )
    payload = jnp.concatenate([sent_pages, own_rows], axis=2)
    received = lax.all_to_all(payload, "blk", split_axis=0, concat_axis=0, tiled=True)
    page_part = received[:, :, : per_peer * page_len]
    page_part = page_part.reshape(blocks, kv_heads, per_peer, page_len, 2 * head_size)
    page_part = page_part.transpose(0, 2, 1, 3, 4).reshape(
        blocks * per_peer, kv_heads, page_len, 2 * head_size
    )
    arriving = (myself - starts[:, None]) % blocks + peer_slots * blocks
    present = (arriving < counts[:, None]).reshape(-1)
    order_rank = jnp.cumsum(present.astype(jnp.int32)) - 1
    choose = present[None, :] & (order_rank[None, :] == jnp.arange(pg, dtype=jnp.int32)[:, None])
    positions = jnp.sum(
        jnp.where(choose, jnp.arange(blocks * per_peer, dtype=jnp.int32)[None, :], 0), axis=1
    )
    compact = page_part[positions]
    compact_valid = jnp.arange(pg, dtype=jnp.int32) * blocks + myself < npages
    gathered = lax.all_gather(compact, "blk", axis=0, tiled=True)
    gathered_valid = (
        jnp.arange(pg, dtype=jnp.int32)[None, :] * blocks + block_ids[:, None] < npages
    ).reshape(-1)
    new_rows = received[:, :, per_peer * page_len :]
    new_rows = new_rows.transpose(1, 0, 2, 3).reshape(kv_heads, blocks * q_rows, 2 * head_size)
    own_pages = compact.transpose(1, 0, 2, 3).reshape(kv_heads, pg * page_len, 2 * head_size)
    entries_a = jnp.concatenate([new_rows, own_pages], axis=1)
    row_source = jnp.repeat(block_ids, q_rows)
    key_pos = jnp.sum(
        jnp.where(row_source[:, None] == block_ids[None, :], block_offsets[None, :], 0), axis=1
    ) * q_rows + jnp.tile(jnp.arange(q_rows, dtype=jnp.int32), blocks)
    visible_new = key_pos[None, :] <= query_pos[:, None]
    visible_own = jnp.broadcast_to(
        jnp.repeat(compact_valid, page_len)[None, :], (query_span, pg * page_len)
    )
    visible_a = jnp.concatenate([visible_new, visible_own], axis=1)[None]
    running = (
        jnp.full((kv_heads, query_span), -1e30, jnp.float32),
        jnp.zeros((kv_heads, query_span), jnp.float32),
        jnp.zeros((kv_heads, query_span, head_size), jnp.float32),
    )
    running = attend(
        running,
        queries,
        entries_a[..., :head_size],
        entries_a[..., head_size:],
        visible_a,
        head_size,
    )
    page_block = jnp.repeat(block_ids, pg)
    use_page = gathered_valid & (page_block != myself)
    entries_b = gathered.transpose(1, 0, 2, 3).reshape(
        kv_heads, blocks * pg * page_len, 2 * head_size
    )
    visible_b = jnp.repeat(use_page, page_len)[None, None, :]
    running = attend(
        running,
        queries,
        entries_b[..., :head_size],
        entries_b[..., head_size:],
        visible_b,
        head_size,
    )
    maxima, totals, summed = running
    attended = (summed / totals[..., None]).astype(jnp.bfloat16)
    attended = attended.reshape(kv_heads, group_size, q_rows, head_size).transpose(2, 0, 1, 3)
    return attended.reshape(q_rows, kv_heads * group_size * head_size)


def solution(mesh):
    return jax.shard_map(
        local,
        mesh=mesh,
        in_specs=(
            P(("groups", "blk"), "pool"),
            P(("groups", "blk"), "pool", None),
            P(("groups", "blk"), "pool", None, None),
            P("groups"),
            P("groups"),
        ),
        out_specs=P(("groups", "blk"), "pool"),
        check_vma=False,
    )
```

profile of v0, /device:TPU:0, one launch (start us, length us, event | category | flops | bytes accessed | tf_op | source)
XLA Modules:
  0.0 97.5 jit_solution(11759745901006424764)
XLA Ops:
  6.5 0.0 copy-start.1
  6.5 0.0 copy-start
  6.5 0.7 and_select_fusion.3
  7.3 0.7 convert_bitcast_fusion
  7.9 0.2 reduce-window.21
  8.1 0.1 convert_reduce_fusion
  8.2 0.2 reduce-window.22
  8.4 1.4 %fusion.35 = (s32[]{:T(128)}, s32[]{:T(128)}) fusion(s32[4]{0:T(128)} %param.9, s32[]{:T(128)S(6)} %axis_index.15, s32[4]{0:T(128)S(1)} %convert_reduce_fusion, s32[4,1]{0,1:T(1,128)S(1)} %reduce-window.22), kind=kLoop, calls=%fused_computation.78 | loop fusion | flops 22 | bytes 60 | tf_op jit(solution)/shard_map/reduce_sum | solution.py:39
  9.8 0.7 and_select_fusion.4
  10.5 0.2 select_reduce_fusion.1
  10.7 0.9 copy.22
  11.6 2.8 %gather_fusion = bf16[4,2,128,256]{3,2,1,0:T(8,128)(2,1)S(1)} fusion(bf16[32,2,128,256]{3,2,1,0:T(8,128)(2,1)} %param.7, s32[1024]{0:T(1024)S(1)} %pad_clamp_fusion.1), kind=kCustom, calls=%fused_computation | custom fusion | bytes 1048592 | tf_op jit(solution)/shard_map/gather | solution.py:59
  14.4 1.1 %pad_maximum_fusion = bf16[4,2,256,256]{3,2,1,0:T(8,128)(2,1)} fusion(bf16[4,2,128,256]{3,2,1,0:T(8,128)(2,1)S(1)} %broadcast_in_dim.150, bf16[4,2,128,256]{3,2,1,0:T(8,128)(2,1)S(1)} %gather_fusion), kind=kLoop, calls=%fused_computation.23 | loop fusion | flops 2097152 | bytes 2097152 | tf_op jit(solution)/shard_map/concatenate | solution.py:66
  15.5 6.3 %all-to-all-start = ((bf16[4,2,256,256]{3,2,1,0:T(8,128)(2,1)}), bf16[4,2,256,256]{3,2,1,0:T(8,128)(2,1)S(1)}, u32[]{:S(2)}, u32[]{:S(2)}) async-start(bf16[4,2,256,256]{3,2,1,0:T(8,128)(2,1)} %pad_maximum_fusion), calls=%async_computation | async-start | bytes 2097152 | tf_op jit(solution)/shard_map/all_to_all | solution.py:67
  21.8 0.0 all-gather.3.cloned.1.call-start
  21.9 0.1 and.99
  21.9 0.2 reduce-window.23
  22.1 0.0 copy-done
  22.1 0.1 copy.32
  22.2 0.1 copy.25
  22.4 0.1 broadcast_bitcast_fusion.2
  23.2 0.1 fusion.33
  23.3 0.0 copy-done.1
  23.3 0.1 select_reduce_fusion
  23.4 24.1 %all-to-all-done = bf16[4,2,256,256]{3,2,1,0:T(8,128)(2,1)S(1)} async-done(((bf16[4,2,256,256]{3,2,1,0:T(8,128)(2,1)}), bf16[4,2,256,256]{3,2,1,0:T(8,128)(2,1)S(1)}, u32[]{:S(2)}, u32[]{:S(2)}) %all-to-all-start) | async-done | bytes 1048608 | tf_op jit(solution)/shard_map/all_to_all | solution.py:67
  47.6 0.1 fusion.51
  47.7 1.3 %gather_fusion.1 = bf16[2,2,128,256]{3,2,1,0:T(8,128)(2,1)} fusion(bf16[4,2,128,256]{3,2,1,0:T(8,128)(2,1)S(1)} %get-tuple-element.10, s32[1024]{0:T(1024)S(1)} %pad_clamp_fusion), kind=kCustom, calls=%fused_computation.1 | custom fusion | bytes 524296 | tf_op jit(solution)/shard_map/gather | solution.py:80
  48.9 0.0 all-gather.3.cloned.1.call-update
  48.9 0.1 broadcast_bitcast_fusion.1
  49.0 0.4 broadcast_compare_fusion
  49.4 0.4 pad_add_fusion
  49.8 1.0 copy.24
  50.8 4.0 %fusion.4 = (f32[2,1024]{1,0:T(2,128)S(1)}, f32[2,768,1024]{2,1,0:T(8,128)}) fusion(pred[1024,768]{0,1:T(8,128)(4,1)S(1)} %pad_add_fusion, bf16[2,1024,128]{2,1,0:T(8,128)(2,1)S(1)} %bitcast.92, bf16[2,512,256]{2,1,0:T(8,128)(2,1)S(1)} %bitcast.98, bf16[2,256,256]{2,1,0:T(8,128)(2,1)S(1)} %bitcast.101), kind=kOutput, calls=%fused_computation.11 | convolution fusion | flops 408156160 | bytes 8396800 | tf_op jit(solution)/shard_map/gqd,gkd->gqk/dot_general | solution.py:14
  54.9 21.3 %all-gather.3.cloned.1.call-done = bf16[8,2,128,256]{3,2,1,0:T(8,128)(2,1)} async-done(((bf16[2,2,128,256]{3,2,1,0:T(8,128)(2,1)}), bf16[8,2,128,256]{3,2,1,0:T(8,128)(2,1)}) %all-gather.3.cloned.1.call-update) | async-done | bytes 1048592 | tf_op jit(solution)/shard_map/all_gather | solution.py:82
  76.1 1.3 %copy.27 = bf16[2,8,128,256]{3,2,1,0:T(8,128)(2,1)S(1)} copy(bf16[2,8,128,256]{3,2,0,1:T(8,128)(2,1)} %bitcast.96) | data formatting | bytes 2097152 | tf_op jit(solution)/shard_map/transpose | solution.py:114
  77.4 0.0 slice-start
  77.4 0.0 slice-start.1
  77.5 1.9 %bitcast_reduce_fusion = (f32[2,1024]{1,0:T(2,128)S(1)}, f32[2,1024,1024]{2,1,0:T(8,128)S(1)}) fusion(pred[1024]{0:T(1024)(128)(4,1)S(1)} %broadcast_bitcast_fusion.1, bf16[2,1024,128]{2,1,0:T(8,128)(2,1)S(1)} %bitcast.93, bf16[2,1024,256]{2,1,0:T(8,128)(2,1)S(1)} %bitcast.89), kind=kOutput, calls=%fused_computation.3 | convolution fusion | flops 543160320 | bytes 9446400 | tf_op jit(solution)/shard_map/gqd,gkd->gqk/dot_general | solution.py:14
  79.4 2.5 %fusion.2 = f32[2,1024]{1,0:T(2,128)S(1)} fusion(f32[2,1024,1024]{2,1,0:T(8,128)S(1)} %get-tuple-element.18, f32[2,1024]{1,0:T(2,128)S(1)} %get-tuple-element.13, pred[1024]{0:T(1024)(128)(4,1)S(1)} %broadcast_bitcast_fusion.1), kind=kLoop, calls=%fused_computation.9 | loop fusion | flops 10483712 | bytes 8406016 | tf_op jit(solution)/shard_map/reduce_sum | solution.py:20
  81.9 0.0 slice-done
  81.9 0.0 slice-done.1
  81.9 1.7 %fusion.5 = f32[2,1024]{1,0:T(2,128)S(1)} fusion(f32[2,768,1024]{2,1,0:T(8,128)S(1)} %bitcast.88, f32[2,1024]{1,0:T(2,128)S(1)} %get-tuple-element.14, pred[1024,768]{0,1:T(8,128)(4,1)S(1)} %pad_add_fusion), kind=kLoop, calls=%fused_computation.12 | loop fusion | flops 7862272 | bytes 7094272 | tf_op jit(solution)/shard_map/reduce_sum | solution.py:20
  83.6 2.8 %fusion.20 = f32[2,1024,128]{2,1,0:T(8,128)S(1)} fusion(f32[2,768,1024]{2,1,0:T(8,128)S(1)} %bitcast.88, f32[2,1024]{1,0:T(2,128)S(1)} %get-tuple-element.14, pred[1024,768]{0,1:T(8,128)(4,1)S(1)} %pad_add_fusion, f32[2,1024]{1,0:T(2,128)S(1)} %get-tuple-element.6, f32[2,1024]{1,0:T(2,128)S(1)} %get-tuple-element.12, ...), kind=kOutput, calls=%fused_computation.22 | convolution fusion | flops 411828224 | bytes 8937472 | tf_op jit(solution)/shard_map/gqk,gkd->gqd/dot_general | solution.py:21
  86.4 3.0 %divide_convert_fusion = bf16[2,1024,128]{2,1,0:T(8,128)(2,1)S(1)} fusion(f32[2,1024,128]{2,1,0:T(8,128)S(1)} %fusion.20, f32[2,1024,1024]{2,1,0:T(8,128)S(1)} %get-tuple-element.18, f32[2,1024]{1,0:T(2,128)S(1)} %get-tuple-element.13, pred[1024]{0:T(1024)(128)(4,1)S(1)} %broadcast_bitcast_fusion.1, bf16[2,1024,256]{2,1,0:T(8,128)(2,1)S(1)} %bitcast.90, ...), kind=kOutput, calls=%fused_computation.24 | convolution fusion | flops 548143104 | bytes 10504192 | tf_op jit(solution)/shard_map/gqk,gkd->gqd/dot_general | solution.py:21
  89.4 0.3 copy.29
  89.8 0.9 copy.35
  (21 shorter events, 0.2 us)
Async XLA Ops:
  6.5 16.8 %copy-start.1 = (s32[4]{0:T(128)S(1)}, s32[4]{0:T(128)}, u32[]{:S(2)}) copy-start(s32[4]{0:T(128)} %param.9) | copy-start | bytes 52
  6.5 15.6 %copy-start = (bf16[128,2048]{1,0:T(8,128)(2,1)S(1)}, bf16[128,2048]{1,0:T(8,128)(2,1)}, u32[]{:S(2)}) copy-start(bf16[128,2048]{1,0:T(8,128)(2,1)} %param.5) | copy-start | bytes 1572868
  15.5 32.0 %all-to-all-start = ((bf16[4,2,256,256]{3,2,1,0:T(8,128)(2,1)}), bf16[4,2,256,256]{3,2,1,0:T(8,128)(2,1)S(1)}, u32[]{:S(2)}, u32[]{:S(2)}) async-start(bf16[4,2,256,256]{3,2,1,0:T(8,128)(2,1)} %pad_maximum_fusion), calls=%async_computation | async-start | bytes 2097152 | tf_op jit(solution)/shard_map/all_to_all | solution.py:67
  21.8 54.3 %all-gather.3.cloned.1.call-start = ((), (), s32[]{:S(2)}) async-start(), calls=%async_computation.1 | async-start | bytes 1310720 | tf_op jit(solution)/shard_map/all_gather | solution.py:82
  77.4 4.5 %slice-start = ((s8[6291456]{0:T(1024)(128)(4,1)}), s8[4194304]{0:T(1024)(128)(4,1)S(1)}, s32[]{:S(2)}) async-start(s8[6291456]{0:T(1024)(128)(4,1)} %bitcast.87), calls=%async_computation.2 | async-start | bytes 8388608
  77.4 4.5 %slice-start.1 = ((s8[6291456]{0:T(1024)(128)(4,1)}), s8[2097152]{0:T(1024)(128)(4,1)S(1)}, s32[]{:S(2)}) async-start(s8[6291456]{0:T(1024)(128)(4,1)} %bitcast.87), calls=%async_computation.3 | async-start | bytes 4194304
Sparse Core Ops, SparseCore 0:
  49.1 27.0 all-gather.2
where the time goes:
time: 97.9 us; the launch traced here: 97.5 us
  waiting for transfers between devices  45.4 us (46%)
  between operations  14.3 us (15%)
  matrix products  11.7 us (12%)
  other arithmetic  10.6 us (11%)
  local copies, waits for them, and re-layouts  9.17 us (9%)
  starting transfers between devices  6.32 us (6%)
    all_to_all x1, waiting for transfers between devices, local(): lax.all_to_all(payload, 'blk', split_axis=0, concat_axis=0, tiled=True)  24.1 us
    all_gather x1, waiting for transfers between devices, local(): gathered = lax.all_gather(compact, 'blk', axis=0, tiled=True)  21.3 us
    all_to_all x1, starting transfers between devices, local(): lax.all_to_all(payload, 'blk', split_axis=0, concat_axis=0, tiled=True)  6.32 us
    dot_general x2, matrix products, attend(): jnp.einsum('gqd,gkd->gqk', queries, keys, preferred_element_type=jnp.floa...  5.92 us
    dot_general x2, matrix products, attend(): jnp.einsum('gqk,gkd->gqd', weights.astype(jnp.bfloat16), values, preferre...  5.81 us
    reduce_sum x2, other arithmetic, attend(): totals = totals * factor + jnp.sum(weights, axis=2)  4.16 us
    gather x1, local copies, waits for them, and re-layouts, local(): kv_cache[chosen]  2.77 us
  transfers between devices with their start and end apart: 2, of which 2 were waited for; matrix products, arithmetic and copies ran while one was open for 7% of the time, Pallas kernels for 0%

commit v1 on v0

--- a/solution.py
+++ b/solution.py
@@ -79,7 +79,14 @@
     )
     compact = page_part[positions]
     compact_valid = jnp.arange(pg, dtype=jnp.int32) * blocks + myself < npages
-    gathered = lax.all_gather(compact, "blk", axis=0, tiled=True)
+    peers = lax.axis_size("blk")
+    right = [(i, (i + 1) % peers) for i in range(peers)]
+    pieces = [compact]
+    for reach in range(1, peers):
+        pieces = [lax.ppermute(pieces[0], "blk", right), *pieces]
+    whole = jnp.concatenate(pieces, axis=0)
+    shift = (lax.axis_index("blk") + 1) * pieces[-1].shape[0]
+    gathered = jnp.roll(whole, shift, axis=0)
     gathered_valid = (
         jnp.arange(pg, dtype=jnp.int32)[None, :] * blocks + block_ids[:, None] < npages
     ).reshape(-1)

time: 97.9 us -> 81.4 us (0.83)
  between operations: 14.3 us -> 0.93 us
  local copies, waits for them, and re-layouts: 9.17 us -> 6.55 us
  matrix products: 11.7 us -> 9.38 us
  waiting for transfers between devices: 45.4 us -> 46.5 us
    ppermute x0 -> x3, waiting for transfers between devices: none -> 22.8 us  [local(): pieces = [lax.ppermute(pieces[0], 'blk', right), *pieces]]
    all_gather x1 -> x0, waiting for transfers between devices: 21.3 us -> none  [local(): gathered = lax.all_gather(compact, 'blk', axis=0, tiled=True)]
    dot_general x2, matrix products: 5.92 us -> 3.29 us  [attend(): jnp.einsum('gqd,gkd->gqk', queries, keys, preferred_element_type=jnp.floa...]
    transpose x1 -> x2, local copies, waits for them, and re-layouts: 1.29 us -> 0.19 us  [local(): gathered.transpose(1, 0, 2, 3)]
  transfers between devices with their start and end apart: 2 -> 4, of which waited for: 2 -> 4; matrix products, arithmetic and copies ran while one was open for 7% -> 5% of each run, Pallas kernels for 0% -> 0%
where the time goes in v1:
time: 81.4 us; the launch traced here: 81.1 us
  waiting for transfers between devices  46.5 us (57%)
  other arithmetic  11.4 us (14%)
  matrix products  9.38 us (12%)
  local copies, waits for them, and re-layouts  6.55 us (8%)
  starting transfers between devices  6.38 us (8%)
  between operations  0.93 us (1%)
    all_to_all x1, waiting for transfers between devices, local(): lax.all_to_all(payload, 'blk', split_axis=0, concat_axis=0, tiled=True)  23.8 us
    ppermute x3, waiting for transfers between devices, local(): pieces = [lax.ppermute(pieces[0], 'blk', right), *pieces]  22.8 us
    all_to_all x1, starting transfers between devices, local(): lax.all_to_all(payload, 'blk', split_axis=0, concat_axis=0, tiled=True)  6.32 us
    dot_general x2, matrix products, attend(): jnp.einsum('gqk,gkd->gqd', weights.astype(jnp.bfloat16), values, preferre...  6.09 us
    reduce_sum x2, other arithmetic, attend(): totals = totals * factor + jnp.sum(weights, axis=2)  4.22 us
    dot_general x2, matrix products, attend(): jnp.einsum('gqd,gkd->gqk', queries, keys, preferred_element_type=jnp.floa...  3.29 us
    gather x1, local copies, waits for them, and re-layouts, local(): kv_cache[chosen]  2.77 us
  transfers between devices with their start and end apart: 4, of which 4 were waited for; matrix products, arithmetic and copies ran while one was open for 5% of the time, Pallas kernels for 0%

profile of v1, /device:TPU:0, one launch (start us, length us, event | category | flops | bytes accessed | tf_op | source)
XLA Modules:
  0.0 81.1 jit_solution(3042054616523214130)
XLA Ops:
  0.0 0.0 copy-start
  0.0 0.7 and_select_fusion.3
  0.7 0.7 convert_bitcast_fusion
  1.4 0.2 reduce-window.21
  1.6 0.1 convert_reduce_fusion
  1.7 0.2 reduce-window.22
  1.9 1.4 %fusion.35 = (s32[]{:T(128)}, s32[]{:T(128)}) fusion(s32[4]{0:T(128)} %param.9, s32[]{:T(128)S(6)} %axis_index.19, s32[4]{0:T(128)S(1)} %convert_reduce_fusion, s32[4,1]{0,1:T(1,128)S(1)} %reduce-window.22), kind=kLoop, calls=%fused_computation.87 | loop fusion | flops 22 | bytes 60 | tf_op jit(solution)/shard_map/reduce_sum | solution.py:39
  3.3 0.7 and_select_fusion.4
  4.0 0.2 select_reduce_fusion.1
  4.2 0.9 %copy.14 = bf16[2,128,256]{2,1,0:T(8,128)(2,1)S(1)} copy(bf16[2,128,256]{2,0,1:T(2,128)(2,1)} %bitcast.101) | data formatting | bytes 262144 | tf_op jit(solution)/shard_map/transpose | solution.py:64
  5.1 2.8 %gather_fusion = bf16[4,2,128,256]{3,2,1,0:T(8,128)(2,1)S(1)} fusion(bf16[32,2,128,256]{3,2,1,0:T(8,128)(2,1)} %param.7, s32[1024]{0:T(1024)S(1)} %pad_clamp_fusion.1), kind=kCustom, calls=%fused_computation | custom fusion | bytes 1048592 | tf_op jit(solution)/shard_map/gather | solution.py:59
  7.9 1.1 %pad_maximum_fusion = bf16[4,2,256,256]{3,2,1,0:T(8,128)(2,1)} fusion(bf16[4,2,128,256]{3,2,1,0:T(8,128)(2,1)S(1)} %broadcast_in_dim.150, bf16[4,2,128,256]{3,2,1,0:T(8,128)(2,1)S(1)} %gather_fusion), kind=kLoop, calls=%fused_computation.23 | loop fusion | flops 2097152 | bytes 2097152 | tf_op jit(solution)/shard_map/concatenate | solution.py:66
  9.0 6.3 %all-to-all-start = ((bf16[4,2,256,256]{3,2,1,0:T(8,128)(2,1)}), bf16[4,2,256,256]{3,2,1,0:T(8,128)(2,1)S(1)}, u32[]{:S(2)}, u32[]{:S(2)}) async-start(bf16[4,2,256,256]{3,2,1,0:T(8,128)(2,1)} %pad_maximum_fusion), calls=%async_computation | async-start | bytes 2097152 | tf_op jit(solution)/shard_map/all_to_all | solution.py:67
  15.3 0.2 reduce-window.23
  16.2 0.1 and.105
  16.3 0.1 fusion.33
  16.4 0.7 select_reduce_fusion
  17.2 0.1 broadcast_bitcast_fusion.1
  17.3 23.8 %all-to-all-done = bf16[4,2,256,256]{3,2,1,0:T(8,128)(2,1)S(1)} async-done(((bf16[4,2,256,256]{3,2,1,0:T(8,128)(2,1)}), bf16[4,2,256,256]{3,2,1,0:T(8,128)(2,1)S(1)}, u32[]{:S(2)}, u32[]{:S(2)}) %all-to-all-start) | async-done | bytes 1048608 | tf_op jit(solution)/shard_map/all_to_all | solution.py:67
  41.0 0.1 fusion.51
  41.1 0.6 gather_fusion.1
  41.7 0.1 collective-permute-start
  41.8 0.1 broadcast_bitcast_fusion.2
  41.8 0.0 copy-done
  41.8 0.1 copy.24
  42.0 0.1 copy.17
  42.1 0.4 broadcast_compare_fusion
  42.5 8.3 %collective-permute-done = bf16[2,2,128,256]{3,2,1,0:T(8,128)(2,1)S(1)} collective-permute-done((bf16[2,2,128,256]{3,2,1,0:T(8,128)(2,1)S(1)}, bf16[2,2,128,256]{3,2,1,0:T(8,128)(2,1)S(1)}, u32[]{:S(2)}, u32[]{:S(2)}) %collective-permute-start) | collective-permute-done | bytes 262176 | tf_op jit(solution)/shard_map/ppermute | solution.py:86
  50.8 0.0 collective-permute-start.1
  50.8 0.4 pad_add_fusion
  51.3 7.7 %collective-permute-done.1 = bf16[2,2,128,256]{3,2,1,0:T(8,128)(2,1)S(1)} collective-permute-done((bf16[2,2,128,256]{3,2,1,0:T(8,128)(2,1)S(1)}, bf16[2,2,128,256]{3,2,1,0:T(8,128)(2,1)S(1)}, u32[]{:S(2)}, u32[]{:S(2)}) %collective-permute-start.1) | collective-permute-done | bytes 262176 | tf_op jit(solution)/shard_map/ppermute | solution.py:86
  59.0 0.0 collective-permute-start.2
  59.0 1.4 %fusion.4 = (f32[2,1024]{1,0:T(2,128)S(1)}, f32[2,768,1024]{2,1,0:T(8,128)S(1)}) fusion(pred[1024,768]{0,1:T(8,128)(4,1)S(1)} %pad_add_fusion, bf16[2,1024,128]{2,1,0:T(8,128)(2,1)S(1)} %bitcast.91, bf16[2,512,256]{2,1,0:T(8,128)(2,1)S(1)} %bitcast.96, bf16[2,256,256]{2,1,0:T(8,128)(2,1)S(1)} %bitcast.99), kind=kOutput, calls=%fused_computation.11 | convolution fusion | flops 408156160 | bytes 8396800 | tf_op jit(solution)/shard_map/gqd,gkd->gqk/dot_general | solution.py:14
  60.4 6.8 %collective-permute-done.2 = bf16[2,2,128,256]{3,2,1,0:T(8,128)(2,1)S(1)} collective-permute-done((bf16[2,2,128,256]{3,2,1,0:T(8,128)(2,1)S(1)}, bf16[2,2,128,256]{3,2,1,0:T(8,128)(2,1)S(1)}, u32[]{:S(2)}, u32[]{:S(2)}) %collective-permute-start.2) | collective-permute-done | bytes 262176 | tf_op jit(solution)/shard_map/ppermute | solution.py:86
  67.4 0.1 dynamic-slice_bitcast_fusion
  67.5 0.1 copy.19
  67.6 1.9 %bitcast_reduce_fusion = (f32[2,1024]{1,0:T(2,128)S(1)}, f32[2,1024,1024]{2,1,0:T(8,128)S(1)}) fusion(pred[1024]{0:T(1024)(128)(4,1)S(1)} %broadcast_bitcast_fusion.1, bf16[2,1024,128]{2,1,0:T(8,128)(2,1)S(1)} %bitcast.92, bf16[2,1024,256]{2,1,0:T(8,128)(2,1)S(1)} %bitcast.89), kind=kOutput, calls=%fused_computation.3 | convolution fusion | flops 543160320 | bytes 9446400 | tf_op jit(solution)/shard_map/gqd,gkd->gqk/dot_general | solution.py:14
  69.5 2.6 %fusion.2 = f32[2,1024]{1,0:T(2,128)S(1)} fusion(f32[2,1024,1024]{2,1,0:T(8,128)S(1)} %get-tuple-element.18, f32[2,1024]{1,0:T(2,128)S(1)} %get-tuple-element.13, pred[1024]{0:T(1024)(128)(4,1)S(1)} %broadcast_bitcast_fusion.1), kind=kLoop, calls=%fused_computation.9 | loop fusion | flops 10483712 | bytes 8406016 | tf_op jit(solution)/shard_map/reduce_sum | solution.py:20
  72.1 1.7 %fusion.5 = f32[2,1024]{1,0:T(2,128)S(1)} fusion(f32[2,768,1024]{2,1,0:T(8,128)S(1)} %get-tuple-element.16, f32[2,1024]{1,0:T(2,128)S(1)} %get-tuple-element.14, pred[1024,768]{0,1:T(8,128)(4,1)S(1)} %pad_add_fusion), kind=kLoop, calls=%fused_computation.12 | loop fusion | flops 7862272 | bytes 7094272 | tf_op jit(solution)/shard_map/reduce_sum | solution.py:20
  73.7 2.9 %fusion.20 = f32[2,1024,128]{2,1,0:T(8,128)S(1)} fusion(f32[2,768,1024]{2,1,0:T(8,128)S(1)} %get-tuple-element.16, f32[2,1024]{1,0:T(2,128)S(1)} %get-tuple-element.14, pred[1024,768]{0,1:T(8,128)(4,1)S(1)} %pad_add_fusion, f32[2,1024]{1,0:T(2,128)S(1)} %get-tuple-element.6, f32[2,1024]{1,0:T(2,128)S(1)} %get-tuple-element.12, ...), kind=kOutput, calls=%fused_computation.22 | convolution fusion | flops 411828224 | bytes 8937472 | tf_op jit(solution)/shard_map/gqk,gkd->gqd/dot_general | solution.py:21
  76.7 3.2 %divide_convert_fusion = bf16[2,1024,128]{2,1,0:T(8,128)(2,1)S(1)} fusion(f32[2,1024,128]{2,1,0:T(8,128)S(1)} %fusion.20, f32[2,1024,1024]{2,1,0:T(8,128)S(1)} %get-tuple-element.18, f32[2,1024]{1,0:T(2,128)S(1)} %get-tuple-element.13, pred[1024]{0:T(1024)(128)(4,1)S(1)} %broadcast_bitcast_fusion.1, bf16[2,1024,256]{2,1,0:T(8,128)(2,1)S(1)} %bitcast.90, ...), kind=kOutput, calls=%fused_computation.24 | convolution fusion | flops 548143104 | bytes 10504192 | tf_op jit(solution)/shard_map/gqk,gkd->gqd/dot_general | solution.py:21
  79.8 0.3 copy.21
  80.2 0.9 %copy.27 = bf16[16,8,16,128]{3,1,2,0:T(8,128)(2,1)} copy(bf16[16,8,16,128]{3,2,1,0:T(8,128)(2,1)S(1)} %bitcast.93) | data formatting | bytes 1048576
  (29 shorter events, 0.4 us)
Async XLA Ops:
  0.0 41.8 %copy-start = (bf16[128,2048]{1,0:T(8,128)(2,1)S(1)}, bf16[128,2048]{1,0:T(8,128)(2,1)}, u32[]{:S(2)}) copy-start(bf16[128,2048]{1,0:T(8,128)(2,1)} %param.5) | copy-start | bytes 1572868
  9.0 32.0 %all-to-all-start = ((bf16[4,2,256,256]{3,2,1,0:T(8,128)(2,1)}), bf16[4,2,256,256]{3,2,1,0:T(8,128)(2,1)S(1)}, u32[]{:S(2)}, u32[]{:S(2)}) async-start(bf16[4,2,256,256]{3,2,1,0:T(8,128)(2,1)} %pad_maximum_fusion), calls=%async_computation | async-start | bytes 2097152 | tf_op jit(solution)/shard_map/all_to_all | solution.py:67
  41.7 9.1 %collective-permute-start = (bf16[2,2,128,256]{3,2,1,0:T(8,128)(2,1)S(1)}, bf16[2,2,128,256]{3,2,1,0:T(8,128)(2,1)S(1)}, u32[]{:S(2)}, u32[]{:S(2)}) collective-permute-start(bf16[2,2,128,256]{3,2,1,0:T(8,128)(2,1)S(1)} %gather_fusion.1), channel_id=1, source_target_pairs={{0,4},{4,8},{8,12},{12,0},{1,5},{5,9},{9,13},{13,1},{2,6},{6,10},{... | collective-permute-start | bytes 786440 | tf_op jit(solution)/shard_map/ppermute | solution.py:86
  50.8 8.2 %collective-permute-start.1 = (bf16[2,2,128,256]{3,2,1,0:T(8,128)(2,1)S(1)}, bf16[2,2,128,256]{3,2,1,0:T(8,128)(2,1)S(1)}, u32[]{:S(2)}, u32[]{:S(2)}) collective-permute-start(bf16[2,2,128,256]{3,2,1,0:T(8,128)(2,1)S(1)} %collective-permute-done), channel_id=1, source_target_pairs={{0,4},{4,8},{8,12},{12,0},{1,5},{5,9},{9,13},{13,1},{2,6},{6,10},{... | collective-permute-start | bytes 786440 | tf_op jit(solution)/shard_map/ppermute | solution.py:86
  59.0 8.2 %collective-permute-start.2 = (bf16[2,2,128,256]{3,2,1,0:T(8,128)(2,1)S(1)}, bf16[2,2,128,256]{3,2,1,0:T(8,128)(2,1)S(1)}, u32[]{:S(2)}, u32[]{:S(2)}) collective-permute-start(bf16[2,2,128,256]{3,2,1,0:T(8,128)(2,1)S(1)} %collective-permute-done.1), channel_id=1, source_target_pairs={{0,4},{4,8},{8,12},{12,0},{1,5},{5,9},{9,13},{13,1},{2,6},{6,10},{... | collective-permute-start | bytes 786440 | tf_op jit(solution)/shard_map/ppermute | solution.py:86
